TPU v7x, 256 devices: a whole 4x4x8 slice. The times are simulated.
256 devices in a mesh: wall: 8 (over y_lo, x), stream: 32 (over z, y_hi, core).
Axes of the slice: x: 4, y: 4 (y_hi: 2, y_lo: 2; y = y_hi * 2 + y_lo), z: 8, core: 2. Of those that a mesh axis runs over, the one named last changes fastest.
Arguments:
- velocity: float32 [3, 64, 512, 128], P(None, 'wall', 'stream'), may hold values from -6 to 6
- sample_block: int32 [8, 256], P('wall', 'stream'), may hold values from 0 to 127
- sample_member: int32 [8, 256, 1], P('wall', 'stream'), may hold values from 0 to 7; in each aligned block of 8 rows (0 to 7, 8 to 15, ..., all dimensions but the last counted through in order) at most 2 rows name the same one
- k_first: bfloat16 [8, 54, 64], P('wall'), may hold values from -6 to 6
- k_second: bfloat16 [8, 27, 64, 64], P('wall'), may hold values from -6 to 6
- w_hidden: bfloat16 [8, 2048, 2048], P('wall'), may hold values from -6 to 6
- w_out: bfloat16 [8, 2048, 2], P('wall'), may hold values from -6 to 6
Outputs:
- new_field: float32 [3, 64, 512, 128], P(None, 'wall', 'stream')
- stress: float32 [2, 8, 256], P(None, 'wall', 'stream')
- new_k_first: float32 [8, 54, 64], P('wall')
- new_k_second: float32 [8, 27, 64, 64], P('wall')
- new_w_hidden: float32 [8, 2048, 2048], P('wall', 'stream')
- new_w_out: float32 [8, 2048, 2], P('wall')
Inputs may be any that keep to these rules, and one draw needn't show every extreme that they name: `sample_member`: in the list of one slab at most 2 samples name the same member; in every draw some slab names some member exactly 2 times.
All inputs are finite; a program needn't handle non-finite values.
Results may differ from a plain program's by a relative error of at most 0.0064.
Values may be sent and summed in bfloat16 or wider, within the bound.
No kernel may reach another device: no remote copies, remote signals or barrier semaphores. Data moves between devices by JAX's collectives and lax.ppermute only.
A program may use at most 128 MiB of HBM per device.

v0:
```python
import math
import jax
import jax.numpy as jnp
import numpy as np
from jax import lax
from jax.sharding import Mesh
from jax.sharding import PartitionSpec as P

P_SIZE = 8
PY = 4
PX = 4
PZ = 8
CH = 64
CAP = 2
FEATS = 2048
STREAM = ("stream_0", "stream_1", "stream_2")
highest = lax.Precision.HIGHEST
time_step = 0.005
relax_rate = 20.0
viscosity = 0.3
learn_rate = 0.5
rms_eps = 1e-06


def extended(shard, sides, width):
    edges = {}
    for axis, dim in sides:
        size, length = (lax.axis_size(axis), shard.shape[dim])
        up = [(i, (i + 1) % size) for i in range(size)]
        last = lax.slice_in_dim(shard, length - width, length, axis=dim)
        first = lax.slice_in_dim(shard, 0, width, axis=dim)
        edges[dim] = (
            lax.ppermute(last, axis, up),
            lax.ppermute(first, axis, [(b, a) for a, b in up]),
        )
    done = []
    for _, dim in sides:
        low, high = edges[dim]
        around = [(width, width) if d in done else (0, 0) for d in range(shard.ndim)]
        shard = jnp.concatenate([jnp.pad(low, around), shard, jnp.pad(high, around)], axis=dim)
        done.append(dim)
    return shard


def in_one_piece(arrays, axis, split_dim, concat_dim, along):
    widths = [math.prod(a.shape[along:]) for a in arrays]
    both = jnp.concatenate(
        [a.reshape(*a.shape[:along], w) for a, w in zip(arrays, widths)], axis=along
    )
    whole = lax.all_to_all(both, axis, split_axis=split_dim, concat_axis=concat_dim, tiled=True)
    tiles = jnp.split(whole, [sum(widths[:k]) for k in range(1, len(widths))], axis=along)
    return tuple((b.reshape(*whole.shape[:along], *a.shape[along:]) for a, b in zip(arrays, tiles)))


def joined_along(tiles, dim):
    lengths = list(tiles.shape[1:])
    lengths[dim] *= tiles.shape[0]
    return jnp.moveaxis(tiles, 0, dim).reshape(lengths)


def gather_in_order(shard, axes, order):
    tiles = shard
    for k in order:
        tiles = lax.all_gather(tiles, axes[k])
    done = order[::-1]
    back = [done.index(k) for k in range(len(axes))]
    tiles = tiles.transpose(*back, *range(len(axes), tiles.ndim))
    return tiles.reshape(-1, *shard.shape)


def gathered_by_axis(shard, axes, order, dim):
    return joined_along(gather_in_order(shard, axes, order), dim)


def cheb_tables(points):
    order = points - 1
    node_index = np.arange(points)
    nodes = -np.cos(np.pi * node_index / order)
    end_weight = np.where((node_index == 0) | (node_index == order), 2.0, 1.0)
    parity = (-1.0) ** (node_index[:, None] + node_index[None, :])
    offdiag = 1.0 - np.eye(points)
    spread = nodes[:, None] - nodes[None, :] + np.eye(points)
    deriv = end_weight[:, None] / end_weight[None, :] * parity / spread * offdiag
    deriv = deriv - np.eye(points) * deriv.sum(axis=1)[:, None]
    highpass = parity / (order * end_weight[None, :])
    return (deriv, highpass, 0.5 * order * order)


def axis_matrices(count, periodic):
    deriv, highpass, lift_half = cheb_tables(P_SIZE)
    length = count * P_SIZE
    slope = np.kron(np.eye(count), deriv)
    upper = np.kron(np.eye(count), highpass)
    faces = count if periodic else count - 1
    for element in range(faces):
        last_node = element * P_SIZE + P_SIZE - 1
        next_node = (element + 1) % count * P_SIZE
        slope[last_node, next_node] += lift_half
        slope[last_node, last_node] -= lift_half
        slope[next_node, last_node] -= lift_half
        slope[next_node, next_node] += lift_half
    if not periodic:
        slope[0, 0] += lift_half
        slope[length - 1, length - 1] -= lift_half
    paired = jnp.asarray(np.concatenate([slope, upper], axis=0), jnp.float32)
    return (paired, lift_half)


def slot_matrix(members, member_count):
    member_hot = (members[..., None] == jnp.arange(member_count, dtype=jnp.int32)).astype(jnp.int32)
    before = jnp.cumsum(member_hot, axis=-2) - member_hot
    ranks = jnp.sum(before * member_hot, axis=-1)
    slots = members * CAP + ranks
    return (slots[..., None, :] == jnp.arange(member_count * CAP, dtype=jnp.int32)[:, None]).astype(
        jnp.float32
    )


DIMS = ("NDHWC", "DHWIO", "NDHWC")
FILTER_DIMS = ("CDHWN", "IDHWO", "NDHWC")
SAME = ((1, 1), (1, 1), (1, 1))


def silu_slope(value):
    gate = jax.nn.sigmoid(value)
    return gate * (1.0 + value * (1.0 - gate))


def conv_taps(grid, kernel):
    return lax.conv_general_dilated(
        grid, kernel, (1, 1, 1), SAME, dimension_numbers=DIMS, preferred_element_type=jnp.float32
    )


def conv_filter(grid, delta):
    taps = lax.conv_general_dilated(
        grid,
        delta,
        (1, 1, 1),
        SAME,
        dimension_numbers=FILTER_DIMS,
        preferred_element_type=jnp.float32,
    )
    return jnp.moveaxis(taps, 0, 3)


def forward_back(patches, aim_rows, valid, k_first, k_second, w_hidden, w_out):
    batch = patches.shape[0]
    channels = k_second.shape[-1]
    inputs = patches.reshape(batch, 2, PY, PX, PZ).transpose(0, 2, 3, 4, 1)
    first_taps = k_first.reshape(3, 3, 3, 2, channels)
    second_taps = k_second.reshape(3, 3, 3, channels, channels)
    scale_one = 1.0 / math.sqrt(54.0)
    scale_two = 1.0 / math.sqrt(27.0 * channels)
    scale_three = 1.0 / math.sqrt(1.0 * w_hidden.shape[0])
    scale_four = 1.0 / math.sqrt(1.0 * w_hidden.shape[1])
    pre_one = conv_taps(inputs, first_taps) * scale_one
    hidden_one = jax.nn.silu(pre_one).astype(jnp.bfloat16)
    pre_two = conv_taps(hidden_one, second_taps) * scale_two
    pooled = (
        jax.nn.silu(pre_two).reshape(batch, PY // 2, 2, PX // 2, 2, PZ, channels).mean(axis=(2, 4))
    )
    features = pooled.reshape(batch, -1).astype(jnp.bfloat16)
    pre_three = jnp.dot(features, w_hidden, preferred_element_type=jnp.float32) * scale_three
    hidden_three = jax.nn.silu(pre_three).astype(jnp.bfloat16)
    pred = jnp.dot(hidden_three, w_out, preferred_element_type=jnp.float32) * scale_four
    error = valid.astype(jnp.float32)[:, None] * (pred - aim_rows.astype(jnp.float32))
    grad_out = jnp.dot(hidden_three.astype(jnp.float32).T, error, precision=highest) * scale_four
    delta_three = (
        jnp.dot(error, w_out.astype(jnp.float32).T, precision=highest)
        * scale_four
        * silu_slope(pre_three)
    ).astype(jnp.bfloat16)
    back_feat = jnp.dot(delta_three, w_hidden.T, preferred_element_type=jnp.float32) * scale_three
    back_grid = back_feat.reshape(batch, PY // 2, 1, PX // 2, 1, PZ, channels)
    spread_back = (
        jnp.broadcast_to(back_grid, (batch, PY // 2, 2, PX // 2, 2, PZ, channels)).reshape(
            pre_two.shape
        )
        * 0.25
    )
    delta_two = (spread_back * silu_slope(pre_two)).astype(jnp.bfloat16)
    grad_two = (conv_filter(hidden_one, delta_two) * scale_two).reshape(27, channels, channels)
    mirrored = jnp.flip(second_taps, axis=(0, 1, 2)).swapaxes(3, 4)
    back_one = conv_taps(delta_two, mirrored)
    delta_one = (back_one * scale_two * silu_slope(pre_one)).astype(jnp.bfloat16)
    grad_one = (conv_filter(inputs, delta_one) * scale_one).reshape(54, channels)
    return (pred, grad_one, grad_two, grad_out, features, delta_three)


def row_update(weight, grad):
    scale = jnp.sqrt(jnp.mean(grad * grad, axis=-1, keepdims=True) + rms_eps)
    return weight.astype(jnp.float32) - learn_rate * grad / scale


def whole_update(weight, grad):
    scale = jnp.sqrt(jnp.mean(grad * grad) + rms_eps)
    return weight.astype(jnp.float32) - learn_rate * grad / scale


def body(velocity, sample_block, sample_member, k_first, k_second, w_hidden, w_out):
    wall_count = lax.axis_size("wall")
    wall_place = lax.axis_index("wall")
    flow_count = lax.axis_size(STREAM)
    flow_place = lax.axis_index(STREAM)
    padded = extended(velocity, (("wall", 1), (STREAM, 2)), 1)
    keep_low = (wall_place > 0).astype(jnp.float32)
    keep_high = (wall_place < wall_count - 1).astype(jnp.float32)
    below = padded[:, 0, 1:-1, :] * keep_low
    above = padded[:, -1, 1:-1, :] * keep_high
    left_face = padded[:, 1:-1, 0, :]
    right_face = padded[:, 1:-1, -1, :]
    size_y, size_x, size_z = (velocity.shape[1], velocity.shape[2], velocity.shape[3])
    pair_y, lift_half = axis_matrices(size_y // P_SIZE, False)
    pair_x, lift_same = axis_matrices(size_x // P_SIZE, False)
    pair_z, lift_again = axis_matrices(size_z // P_SIZE, True)
    along_y = jnp.einsum("cyxz,wy->cwxz", velocity, pair_y, precision=highest)
    grad_y = (
        along_y[:, :size_y]
        .at[:, 0]
        .add(-lift_half * below)
        .at[:, size_y - 1]
        .add(lift_half * above)
    )
    high_y = along_y[:, size_y:]
    along_x = jnp.einsum("cyxz,wx->cywz", velocity, pair_x, precision=highest)
    grad_x = (
        along_x[:, :, :size_x]
        .at[:, :, 0]
        .add(-lift_half * left_face)
        .at[:, :, size_x - 1]
        .add(lift_half * right_face)
    )
    high_x = along_x[:, :, size_x:]
    along_z = jnp.einsum("cyxz,wz->cyxw", velocity, pair_z, precision=highest)
    grad_z = along_z[..., :size_z]
    high_z = along_z[..., size_z:]
    advect = velocity[0][None] * grad_x + velocity[1][None] * grad_y + velocity[2][None] * grad_z
    new_field = velocity + time_step * (-advect - relax_rate * (high_x + high_y + high_z))
    rows_y, rows_x, rows_z = (size_y // PY, size_x // PX, size_z // PZ)
    tangent = jnp.stack([velocity[0], velocity[2]]).reshape(2, rows_y, PY, rows_x, PX, rows_z, PZ)
    blocks = tangent.transpose(1, 3, 5, 0, 2, 4, 6).reshape(-1, 2 * PY * PX * PZ)
    slope_wall = jnp.stack([grad_y[0], grad_y[2]]).reshape(2, rows_y, PY, rows_x, PX, rows_z, PZ)
    stress_true = (
        (viscosity * jnp.mean(slope_wall, axis=(2, 4, 6))).transpose(1, 2, 3, 0).reshape(-1, 2)
    )
    picked = sample_block.reshape(-1)
    members = sample_member.reshape(-1)
    patch_rows = jnp.take(blocks, picked, axis=0).astype(jnp.bfloat16)
    aim_rows = jnp.take(stress_true, picked, axis=0).astype(jnp.bfloat16)
    select = slot_matrix(members, wall_count)
    select_half = select.astype(jnp.bfloat16)
    send_rows = jnp.dot(select_half, patch_rows, preferred_element_type=jnp.float32).astype(
        jnp.bfloat16
    )
    send_aims = jnp.dot(select_half, aim_rows, preferred_element_type=jnp.float32).astype(
        jnp.bfloat16
    )
    send_valid = jnp.sum(select, axis=1).astype(jnp.bfloat16)
    recv_rows, recv_aims, recv_valid = in_one_piece(
        (send_rows, send_aims, send_valid), "wall", 0, 0, 1
    )
    pred, grad_one, grad_two, grad_out, features, delta_three = forward_back(
        recv_rows, recv_aims, recv_valid, k_first[0], k_second[0], w_hidden[0], w_out[0]
    )
    back = lax.all_to_all(pred, "wall", split_axis=0, concat_axis=0, tiled=True)
    stress_local = jnp.dot(select.T, back, precision=highest)
    stress = stress_local.T[:, None, :]
    share_rows = FEATS // flow_count
    dense_scale = 1.0 / math.sqrt(1.0 * FEATS)
    columns_here = lax.all_to_all(features, STREAM, split_axis=1, concat_axis=0, tiled=True)
    grad_hidden = (
        jnp.dot(
            columns_here.T,
            gathered_by_axis(delta_three, STREAM, (1, 0, 2), 0),
            preferred_element_type=jnp.float32,
        )
        * dense_scale
    )
    own_rows = lax.dynamic_slice_in_dim(w_hidden[0], flow_place * share_rows, share_rows, 0)
    new_w_hidden = row_update(own_rows, grad_hidden)[None]
    grad_one, grad_two, grad_out = lax.psum((grad_one, grad_two, grad_out), STREAM)
    new_k_second = row_update(k_second[0], grad_two)
    new_k_first = row_update(k_first[0], grad_one)
    new_w_out = whole_update(w_out[0], grad_out)
    return (new_field, stress, new_k_first[None], new_k_second[None], new_w_hidden, new_w_out[None])


def solution(mesh):
    torus = Mesh(
        mesh.devices.reshape(mesh.shape["wall"], 8, 2, 2),
        ("wall", "stream_0", "stream_1", "stream_2"),
    )
    in_specs = (
        P(None, "wall", STREAM, None),
        P("wall", STREAM),
        P("wall", STREAM, None),
        P("wall", None, None),
        P("wall", None, None, None),
        P("wall", None, None),
        P("wall", None, None),
    )
    out_specs = (
        P(None, "wall", STREAM, None),
        P(None, "wall", STREAM),
        P("wall", None, None),
        P("wall", None, None, None),
        P("wall", STREAM, None),
        P("wall", None, None),
    )
    return jax.shard_map(body, mesh=torus, in_specs=in_specs, out_specs=out_specs, check_vma=False)
```

profile of v0, /device:TPU:1, one launch (start us, length us, event | category | flops | bytes accessed | tf_op | source)
XLA Modules:
  0.0 358.8 jit_solution(1956748719228689826)
XLA Ops:
  8.8 2.0 collective-permute-start.2
  10.9 2.4 collective-permute-start.3
  13.2 1.6 fusion.46
  14.8 4.0 %collective-permute-start = (f32[3,8,1,128]{3,2,1,0:T(1,128)}, f32[3,8,1,128]{3,2,1,0:T(1,128)}, u32[]{:S(2)}, u32[]{:S(2)}) collective-permute-start(f32[3,8,1,128]{3,2,1,0:T(1,128)} %get-tuple-element.94), channel_id=1, source_target_pairs={{0,1},{1,2},{2,3},{3,4},{4,5},{5,6},{6,7},{7,8},{8,9},{9,10},{10,1... | collective-permute-start | bytes 36872 | tf_op jit(solution)/shard_map/ppermute | solution.py:33
  20.1 0.9 fusion.44
  21.0 1.5 convolution_bitcast_fusion
  22.5 1.5 fusion.23
  24.0 1.5 convolution_bitcast_fusion.1
  26.2 0.8 select_reduce_fusion
  27.7 1.2 reshape.297
  32.6 2.1 reshape.300
  35.6 0.9 convolution_convert_fusion.1
  37.3 3.3 all-to-all-start
  41.0 4.7 %all-to-all-done = bf16[8,2,259]{2,1,0:T(2,128)(2,1)S(1)} async-done(((bf16[8,2,259]{2,1,0:T(2,128)(2,1)}), bf16[8,2,259]{2,1,0:T(2,128)(2,1)S(1)}, u32[]{:S(2)}, u32[]{:S(2)}) %all-to-all-start) | async-done | bytes 8320 | tf_op jit(solution)/shard_map/all_to_all | solution.py:50
  46.0 0.9 convolution_multiply_fusion.4
  46.9 4.5 %fusion.14 = (f32[16,4,4,8,64]{4,0,3,2,1:T(8,128)}, f32[16,4,4,8,64]{4,0,3,2,1:T(8,128)}) fusion(bf16[3,3,3,64,64]{4,3,2,1,0:T(8,128)(2,1)} %bitcast.138, f32[16,4,4,8,64]{4,0,3,2,1:T(8,128)S(1)} %convolution_multiply_fusion.4), kind=kOutput, calls=%fused_computation.26 | convolution fusion | flops 289669120 | bytes 1794048 | tf_op jit(solution)/shard_map/conv_general_dilated | solution.py:130
  51.4 1.3 reduce_sum.75
  53.1 4.6 %multiply_convert_fusion.3 = (bf16[16,2048]{1,0:T(8,128)(2,1)S(1)}, f32[16,2048]{1,0:T(8,128)S(1)}) fusion(bf16[16,2048]{1,0:T(8,128)(2,1)S(1)} %convert_element_type.116, bf16[1,2048,2048]{2,1,0:T(8,128)(2,1)} %param.23), kind=kOutput, calls=%fused_computation.50 | convolution fusion | flops 134414336 | bytes 8650752 | tf_op jit(solution)/shard_map/dot_general | solution.py:164
  58.6 5.4 %all-gather = bf16[32,2048]{1,0:T(8,128)(2,1)} all-gather(bf16[16,2048]{1,0:T(8,128)(2,1)S(1)} %fusion.11), channel_id=2, replica_groups=mesh['wall'=8,'stream_0'=8,'stream_1'=2,'stream_2'=2] {'stream_1'}, dimensions={0}, use_global_device_ids=true | all-gather | bytes 196608 | tf_op jit(solution)/shard_map/all_gather | solution.py:64
  66.6 5.7 %fusion.8 = f32[16,2048]{1,0:T(8,128)S(1)} fusion(bf16[16,2048]{1,0:T(8,128)(2,1)S(1)} %fusion.11, bf16[1,2048,2048]{2,1,0:T(8,128)(2,1)} %param.23), kind=kOutput, calls=%fused_computation.9 | convolution fusion | flops 134250496 | bytes 8585216 | tf_op jit(solution)/shard_map/dot_general | solution.py:174
  73.1 3.6 %convolution_multiply_fusion.5 = f32[3,3,3,64,64]{4,3,2,1,0:T(8,128)} fusion(bf16[16,4,4,8,64]{4,0,3,2,1:T(8,128)(2,1)S(1)} %multiply_convert_fusion, f32[16,4,4,8,64]{4,0,3,2,1:T(8,128)S(1)} %convolution_multiply_fusion.4), kind=kOutput, calls=%fused_computation.16 | convolution fusion | flops 289124352 | bytes 1228800 | tf_op jit(solution)/shard_map/transpose | solution.py:144
  77.1 4.2 %convolution_multiply_fusion.6 = f32[3,3,3,2,64]{4,3,2,1,0:T(2,128)S(1)} fusion(bf16[16,2,4,4,8]{0,4,3,2,1:T(8,128)(2,1)S(1)} %bitcast.141, bf16[16,4,4,8,64]{4,0,3,2,1:T(8,128)(2,1)S(1)} %multiply_convert_fusion, bf16[3,3,3,64,64]{4,3,2,1,0:T(8,128)(2,1)S(1)} %bitcast.139, f32[16,4,4,8,64]{4,0,3,2,1:T(8,128)S(1)} %convolution_multiply_fusion.4), kind=kOutput, calls=%fused_computation.20 | convolution fusion | flops 298683776 | bytes 1029632 | tf_op jit(solution)/shard_map/transpose | solution.py:144
  81.3 19.8 %all-gather.6.cloned.1.call-done = bf16[16,16,2048]{2,1,0:T(8,128)(2,1)} async-done(((bf16[2,16,2048]{2,1,0:T(8,128)(2,1)}), bf16[16,16,2048]{2,1,0:T(8,128)(2,1)}) %all-gather.6.cloned.1.call-update) | async-done | bytes 1048592 | tf_op jit(solution)/shard_map/all_gather | solution.py:64
  102.0 4.9 %all-to-all-start.1 = ((f32[8,2,2]{1,2,0:T(2,128)}), f32[8,2,2]{1,2,0:T(2,128)S(1)}, u32[]{:S(2)}, u32[]{:S(2)}) async-start(f32[8,2,2]{1,2,0:T(2,128)} %copy.77), calls=%async_computation.1 | async-start | bytes 16384 | tf_op jit(solution)/shard_map/all_to_all | solution.py:266
  107.0 128.6 %all-reduce = (f32[54,64]{1,0:T(8,128)S(1)}, f32[2048,2]{0,1:T(2,128)S(1)}) all-reduce(f32[54,64]{1,0:T(8,128)S(1)} %reshape.304, f32[2048,2]{0,1:T(2,128)S(1)} %convolution_multiply_fusion.1), channel_id=1, replica_groups=mesh['wall'=8,'stream_0'=8,'stream_1'=2,'stream_2'=2] {'stream_0','strea..., use_global_device_ids=true, to_apply=%region_5.6 | all-reduce | flops 7552 | bytes 60416 | tf_op jit(solution)/shard_map/psum | solution.py:282
  239.1 10.2 %all-to-all-start.2 = ((bf16[32,2,512]{2,1,0:T(2,128)(2,1)}), bf16[32,2,512]{2,1,0:T(2,128)(2,1)S(1)}, u32[]{:S(2)}, u32[]{:S(2)}) async-start(bf16[32,2,512]{2,1,0:T(2,128)(2,1)} %reshape.333), calls=%async_computation.2 | async-start | bytes 131072 | tf_op jit(solution)/shard_map/all_to_all | solution.py:271
  250.2 9.0 %all-to-all-done.2 = bf16[32,2,512]{2,1,0:T(2,128)(2,1)S(1)} async-done(((bf16[32,2,512]{2,1,0:T(2,128)(2,1)}), bf16[32,2,512]{2,1,0:T(2,128)(2,1)S(1)}, u32[]{:S(2)}, u32[]{:S(2)}) %all-to-all-start.2) | async-done | bytes 65568 | tf_op jit(solution)/shard_map/all_to_all | solution.py:271
  259.3 84.0 %all-reduce.3.cloned.1.call-done = f32[27,64,64]{2,1,0:T(8,128)} async-done(((f32[27,64,64]{2,1,0:T(8,128)}), f32[27,64,64]{2,1,0:T(8,128)}) %all-reduce.3.cloned.1.call-update) | async-done | bytes 442384 | tf_op jit(solution)/shard_map/psum | solution.py:282
  343.3 1.5 multiply_reduce_fusion
  344.7 2.4 fusion.15
  347.1 1.7 copy.82
  349.5 1.9 fusion.16
  (120 shorter events, 19.6 us)
Async XLA Ops:
  8.0 32.9 %copy-start = (f32[3,8,16,128]{3,2,1,0:T(8,128)S(1)}, f32[3,8,16,128]{3,2,1,0:T(8,128)}, u32[]{:S(2)}) copy-start(f32[3,8,16,128]{3,2,1,0:T(8,128)} %param.18) | copy-start | bytes 589828
  8.0 32.9 %copy-start.9 = (bf16[1,54,64]{2,1,0:T(8,128)(2,1)S(1)}, bf16[1,54,64]{2,1,0:T(8,128)(2,1)}, u32[]{:S(2)}) copy-start(bf16[1,54,64]{2,1,0:T(8,128)(2,1)} %param.21) | copy-start | bytes 20740
  8.8 22.3 %collective-permute-start.2 = (f32[3,1,16,128]{3,2,1,0:T(8,128)S(1)}, f32[3,1,16,128]{3,2,1,0:T(8,128)S(1)}, u32[]{:S(2)}, u32[]{:S(2)}) collective-permute-start(f32[3,1,16,128]{3,2,1,0:T(8,128)S(1)} %get-tuple-element.96), channel_id=1, source_target_pairs={{0,32},{32,64},{64,96},{96,128},{128,160},{160,192},{192,224},{224... | collective-permute-start | bytes 73736 | tf_op jit(solution)/shard_map/ppermute | solution.py:33
  10.9 20.3 %collective-permute-start.3 = (f32[3,1,16,128]{3,2,1,0:T(8,128)S(1)}, f32[3,1,16,128]{3,2,1,0:T(8,128)S(1)}, u32[]{:S(2)}, u32[]{:S(2)}) collective-permute-start(f32[3,1,16,128]{3,2,1,0:T(8,128)S(1)} %get-tuple-element.95), channel_id=1, source_target_pairs={{32,0},{64,32},{96,64},{128,96},{160,128},{192,160},{224,192},{0,2... | collective-permute-start | bytes 73736 | tf_op jit(solution)/shard_map/ppermute | solution.py:34
  14.8 49.3 %collective-permute-start = (f32[3,8,1,128]{3,2,1,0:T(1,128)}, f32[3,8,1,128]{3,2,1,0:T(1,128)}, u32[]{:S(2)}, u32[]{:S(2)}) collective-permute-start(f32[3,8,1,128]{3,2,1,0:T(1,128)} %get-tuple-element.94), channel_id=1, source_target_pairs={{0,1},{1,2},{2,3},{3,4},{4,5},{5,6},{6,7},{7,8},{8,9},{9,10},{10,1... | collective-permute-start | bytes 36872 | tf_op jit(solution)/shard_map/ppermute | solution.py:33
  18.8 46.1 %collective-permute-start.1 = (f32[3,8,1,128]{3,2,1,0:T(1,128)S(1)}, f32[3,8,1,128]{3,2,1,0:T(1,128)}, u32[]{:S(2)}, u32[]{:S(2)}) collective-permute-start(f32[3,8,1,128]{3,2,1,0:T(1,128)S(1)} %get-tuple-element.93), channel_id=1, source_target_pairs={{1,0},{2,1},{3,2},{4,3},{5,4},{6,5},{7,6},{8,7},{9,8},{10,9},{11,1... | collective-permute-start | bytes 36872 | tf_op jit(solution)/shard_map/ppermute | solution.py:34
  20.1 10.4 %copy-start.18 = (pred[8]{0:T(512)(128)(4,1)}, pred[8]{0:T(512)(128)(4,1)S(1)}, u32[]{:S(2)}) copy-start(pred[8]{0:T(512)(128)(4,1)S(1)} %compare_and_fusion) | copy-start | bytes 28
  27.7 23.7 %copy-start.16 = (s32[8]{0:T(128)}, s32[8]{0:T(128)S(1)}, u32[]{:S(2)}) copy-start(s32[8]{0:T(128)S(1)} %multiply_add_fusion) | copy-start | bytes 100
  31.2 0.7 copy-start.1
  37.3 8.3 %all-to-all-start = ((bf16[8,2,259]{2,1,0:T(2,128)(2,1)}), bf16[8,2,259]{2,1,0:T(2,128)(2,1)S(1)}, u32[]{:S(2)}, u32[]{:S(2)}) async-start(bf16[8,2,259]{2,1,0:T(2,128)(2,1)} %pad_maximum_fusion.2), calls=%async_computation | async-start | bytes 24576 | tf_op jit(solution)/shard_map/all_to_all | solution.py:50
  40.7 60.5 %all-gather.6.cloned.1.call-start = ((), (), s32[]{:S(2)}) async-start(), calls=%async_computation.4 | async-start | bytes 1179648 | tf_op jit(solution)/shard_map/all_gather | solution.py:64
  45.9 12.5 %copy-start.12 = (f32[16]{0:T(128)}, f32[16]{0:T(128)S(1)}, u32[]{:S(2)}) copy-start(f32[16]{0:T(128)S(1)} %convert_reduce_fusion) | copy-start | bytes 196
  46.0 5.4 %copy-start.7 = (bf16[16,256]{0,1:T(8,128)(2,1)}, bf16[16,256]{0,1:T(8,128)(2,1)S(1)}, u32[]{:S(2)}) copy-start(bf16[16,256]{0,1:T(8,128)(2,1)S(1)} %copy.74) | copy-start | bytes 24580
  52.7 5.0 %copy-start.10 = (bf16[1,2048,2]{1,2,0:T(2,128)(2,1)S(1)}, bf16[1,2048,2]{1,2,0:T(2,128)(2,1)}, u32[]{:S(2)}) copy-start(bf16[1,2048,2]{1,2,0:T(2,128)(2,1)} %param.24) | copy-start | bytes 24580
  53.1 5.6 %copy-start.14 = (bf16[16,2]{0,1:T(2,128)(2,1)}, bf16[16,2]{0,1:T(2,128)(2,1)S(1)}, u32[]{:S(2)}) copy-start(bf16[16,2]{0,1:T(2,128)(2,1)S(1)} %copy.88) | copy-start | bytes 196
  53.1 12.7 %copy-start.2 = (f32[3,8,16,128]{3,2,1,0:T(8,128)S(1)}, f32[3,8,16,128]{3,2,1,0:T(8,128)}, u32[]{:S(2)}) copy-start(f32[3,8,16,128]{3,2,1,0:T(8,128)} %copy-done.1) | copy-start | bytes 589828
  57.7 0.6 copy-start.5
  64.1 279.2 %all-reduce.3.cloned.1.call-start = ((), (), s32[]{:S(2)}) async-start(), calls=%async_computation.3 | async-start | bytes 1769472 | tf_op jit(solution)/shard_map/psum | solution.py:282
  66.6 6.1 %copy-start.3 = (f32[16,4,4,8,64]{4,0,3,2,1:T(8,128)S(1)}, f32[16,4,4,8,64]{4,0,3,2,1:T(8,128)}, u32[]{:S(2)}) copy-start(f32[16,4,4,8,64]{4,0,3,2,1:T(8,128)} %get-tuple-element.98) | copy-start | bytes 1572868
  72.7 4.4 %copy-start.4 = (bf16[1,27,64,64]{3,2,1,0:T(8,128)(2,1)S(1)}, bf16[1,27,64,64]{3,2,1,0:T(8,128)(2,1)}, u32[]{:S(2)}) copy-start(bf16[1,27,64,64]{3,2,1,0:T(8,128)(2,1)} %param.22) | copy-start | bytes 663556
  72.7 4.4 %copy-start.8 = (bf16[16,256]{0,1:T(8,128)(2,1)S(1)}, bf16[16,256]{0,1:T(8,128)(2,1)}, u32[]{:S(2)}) copy-start(bf16[16,256]{0,1:T(8,128)(2,1)} %copy-done.7) | copy-start | bytes 24580
  76.8 24.4 %copy-start.6 = (bf16[16,2048]{1,0:T(8,128)(2,1)S(1)}, bf16[16,2048]{1,0:T(8,128)(2,1)}, u32[]{:S(2)}) copy-start(bf16[16,2048]{1,0:T(8,128)(2,1)} %copy-done.5) | copy-start | bytes 196612
  76.8 24.4 %copy-start.13 = (f32[16]{0:T(128)S(1)}, f32[16]{0:T(128)}, u32[]{:S(2)}) copy-start(f32[16]{0:T(128)} %copy-done.12) | copy-start | bytes 196
  76.8 24.4 %copy-start.15 = (bf16[16,2]{0,1:T(2,128)(2,1)S(1)}, bf16[16,2]{0,1:T(2,128)(2,1)}, u32[]{:S(2)}) copy-start(bf16[16,2]{0,1:T(2,128)(2,1)} %copy-done.14) | copy-start | bytes 196
  76.8 160.9 %copy-start.11 = (bf16[1,2048,2]{1,2,0:T(2,128)(2,1)S(1)}, bf16[1,2048,2]{1,2,0:T(2,128)(2,1)}, u32[]{:S(2)}) copy-start(bf16[1,2048,2]{1,2,0:T(2,128)(2,1)} %param.24) | copy-start | bytes 24580
  76.8 172.6 %copy-start.17 = (s32[8]{0:T(128)S(1)}, s32[8]{0:T(128)}, u32[]{:S(2)}) copy-start(s32[8]{0:T(128)} %copy-done.16) | copy-start | bytes 100
  76.8 270.3 %all-gather.8.cloned.1.call-start = ((), (), s32[]{:S(2)}) async-start(), calls=%async_computation.5 | async-start | bytes 3145728 | tf_op jit(solution)/shard_map/all_gather | solution.py:64
  102.0 137.1 %all-to-all-start.1 = ((f32[8,2,2]{1,2,0:T(2,128)}), f32[8,2,2]{1,2,0:T(2,128)S(1)}, u32[]{:S(2)}, u32[]{:S(2)}) async-start(f32[8,2,2]{1,2,0:T(2,128)} %copy.77), calls=%async_computation.1 | async-start | bytes 16384 | tf_op jit(solution)/shard_map/all_to_all | solution.py:266
  239.1 20.0 %all-to-all-start.2 = ((bf16[32,2,512]{2,1,0:T(2,128)(2,1)}), bf16[32,2,512]{2,1,0:T(2,128)(2,1)S(1)}, u32[]{:S(2)}, u32[]{:S(2)}) async-start(bf16[32,2,512]{2,1,0:T(2,128)(2,1)} %reshape.333), calls=%async_computation.2 | async-start | bytes 131072 | tf_op jit(solution)/shard_map/all_to_all | solution.py:271
Sparse Core Ops, SparseCore 0:
  64.2 36.9 all-gather.5
  103.1 19.9 all-gather.7
Sparse Core Ops, SparseCore 1:
  76.8 266.4 all-reduce.2
where the time goes:
time: 360 us; the launch traced here: 359 us
  blocking collectives  134 us (37%)
  waiting for transfers between devices  117 us (32%)
  matrix products  31 us (9%)
  starting transfers between devices  27.4 us (8%)
  between operations  16.8 us (5%)
  other arithmetic  16.6 us (5%)
  local copies, waits for them, and re-layouts  15.5 us (4%)
    psum x1, blocking collectives, body(): lax.psum((grad_one, grad_two, grad_out), STREAM)  129 us
    psum x1, waiting for transfers between devices, body(): lax.psum((grad_one, grad_two, grad_out), STREAM)  84 us
    all_gather x2, waiting for transfers between devices, gather_in_order(): tiles = lax.all_gather(tiles, axes[k])  19.8 us
    all_to_all x1, starting transfers between devices, body(): lax.all_to_all(features, STREAM, split_axis=1, concat_axis=0, tiled=True)  10.2 us
    all_to_all x1, waiting for transfers between devices, body(): lax.all_to_all(features, STREAM, split_axis=1, concat_axis=0, tiled=True)  8.98 us
    transpose x2, matrix products, conv_filter(): return jnp.moveaxis(taps, 0, 3)  7.83 us
  transfers between devices with their start and end apart: 10, of which 4 were waited for; matrix products, arithmetic and copies ran while one was open for 16% of the time, Pallas kernels for 0%

commit v1 on v0

--- a/solution.py
+++ b/solution.py
@@ -1,3 +1,4 @@
+import functools
 import math
 import jax
 import jax.numpy as jnp
@@ -20,6 +21,17 @@
 viscosity = 0.3
 learn_rate = 0.5
 rms_eps = 1e-06
+
+
+def supply_outputs_by_axis(field_in, axis_tag, shard_axis):
+    for at in (axis_tag, shard_axis):
+        field_in = jax.lax.psum(field_in, at)
+    return field_in
+
+
+shape_figure = functools.partial(
+    supply_outputs_by_axis, axis_tag="stream_0", shard_axis=("stream_1", "stream_2")
+)
 
 
 def extended(shard, sides, width):
@@ -279,7 +291,7 @@
     )
     own_rows = lax.dynamic_slice_in_dim(w_hidden[0], flow_place * share_rows, share_rows, 0)
     new_w_hidden = row_update(own_rows, grad_hidden)[None]
-    grad_one, grad_two, grad_out = lax.psum((grad_one, grad_two, grad_out), STREAM)
+    grad_one, grad_two, grad_out = shape_figure((grad_one, grad_two, grad_out))
     new_k_second = row_update(k_second[0], grad_two)
     new_k_first = row_update(k_first[0], grad_one)
     new_w_out = whole_update(w_out[0], grad_out)

time: 360 us -> 258 us (0.72)
  blocking collectives: 134 us -> 53.3 us
  waiting for transfers between devices: 117 us -> 100 us
    psum x1 -> x2, blocking collectives: 129 us -> 47.9 us  [supply_outputs_by_axis(): field_in = jax.lax.psum(field_in, at)]
    psum x1 -> x2, waiting for transfers between devices: 84 us -> 52.2 us  [supply_outputs_by_axis(): field_in = jax.lax.psum(field_in, at)]
    all_gather x2, waiting for transfers between devices: 19.8 us -> 32.9 us  [gather_in_order(): tiles = lax.all_gather(tiles, axes[k])]
  transfers between devices with their start and end apart: 10 -> 11, of which waited for: 4 -> 5; matrix products, arithmetic and copies ran while one was open for 16% -> 12% of each run, Pallas kernels for 0% -> 0%
where the time goes in v1:
time: 258 us; the launch traced here: 257 us
  waiting for transfers between devices  100 us (39%)
  blocking collectives  53.3 us (21%)
  matrix products  28.1 us (11%)
  starting transfers between devices  27.8 us (11%)
  other arithmetic  17.4 us (7%)
  local copies, waits for them, and re-layouts  15.5 us (6%)
  between operations  15.1 us (6%)
    psum x2, waiting for transfers between devices, supply_outputs_by_axis(): field_in = jax.lax.psum(field_in, at)  52.2 us
    psum x2, blocking collectives, supply_outputs_by_axis(): field_in = jax.lax.psum(field_in, at)  47.9 us
    all_gather x2, waiting for transfers between devices, gather_in_order(): tiles = lax.all_gather(tiles, axes[k])  32.9 us
    all_to_all x1, waiting for transfers between devices, body(): lax.all_to_all(features, STREAM, split_axis=1, concat_axis=0, tiled=True)  8.98 us
    transpose x2, matrix products, conv_filter(): return jnp.moveaxis(taps, 0, 3)  8.93 us
    all_to_all x1, starting transfers between devices, body(): lax.all_to_all(features, STREAM, split_axis=1, concat_axis=0, tiled=True)  8.47 us
    ppermute x2, starting transfers between devices, extended(): lax.ppermute(last, axis, up)  8.39 us
    dot_general x1, matrix products, forward_back(): jnp.dot(delta_three, w_hidden.T, preferred_element_type=jnp.float32)  5.67 us
  transfers between devices with their start and end apart: 11, of which 5 were waited for; matrix products, arithmetic and copies ran while one was open for 12% of the time, Pallas kernels for 0%

profile of v1, /device:TPU:1, one launch (start us, length us, event | category | flops | bytes accessed | tf_op | source)
XLA Modules:
  0.0 257.5 jit_solution(11953828679941460608)
XLA Ops:
  8.0 2.0 collective-permute-start.2
  10.0 2.3 collective-permute-start.3
  13.7 0.9 fusion.44
  14.6 1.5 fusion.23
  16.8 0.8 select_reduce_fusion
  18.3 1.2 reshape.297
  21.9 1.1 reshape.300
  25.0 3.3 %all-to-all-start = ((bf16[8,2,259]{2,1,0:T(2,128)(2,1)}), bf16[8,2,259]{2,1,0:T(2,128)(2,1)S(1)}, u32[]{:S(2)}, u32[]{:S(2)}) async-start(bf16[8,2,259]{2,1,0:T(2,128)(2,1)} %pad_maximum_fusion.2), calls=%async_computation | async-start | bytes 24576 | tf_op jit(solution)/shard_map/all_to_all | solution.py:62
  28.6 4.7 %all-to-all-done = bf16[8,2,259]{2,1,0:T(2,128)(2,1)S(1)} async-done(((bf16[8,2,259]{2,1,0:T(2,128)(2,1)}), bf16[8,2,259]{2,1,0:T(2,128)(2,1)S(1)}, u32[]{:S(2)}, u32[]{:S(2)}) %all-to-all-start) | async-done | bytes 8320 | tf_op jit(solution)/shard_map/all_to_all | solution.py:62
  34.8 0.9 convolution_multiply_fusion.4
  35.7 3.1 %fusion.14 = (f32[16,4,4,8,64]{4,0,3,2,1:T(8,128)S(1)}, f32[16,4,4,8,64]{4,0,3,2,1:T(8,128)}) fusion(bf16[3,3,3,64,64]{4,3,2,1,0:T(8,128)(2,1)S(1)} %bitcast.139, f32[16,4,4,8,64]{4,0,3,2,1:T(8,128)S(1)} %convolution_multiply_fusion.4), kind=kOutput, calls=%fused_computation.26 | convolution fusion | flops 289669120 | bytes 1794048 | tf_op jit(solution)/shard_map/conv_general_dilated | solution.py:142
  39.3 4.6 %multiply_convert_fusion.3 = (bf16[16,2048]{1,0:T(8,128)(2,1)S(1)}, f32[16,2048]{1,0:T(8,128)S(1)}) fusion(bf16[16,2048]{1,0:T(8,128)(2,1)S(1)} %convert_element_type.116, bf16[1,2048,2048]{2,1,0:T(8,128)(2,1)} %param.23), kind=kOutput, calls=%fused_computation.50 | convolution fusion | flops 134414336 | bytes 8650752 | tf_op jit(solution)/shard_map/dot_general | solution.py:176
  44.8 5.7 %fusion.8 = f32[16,2048]{1,0:T(8,128)S(1)} fusion(bf16[16,2048]{1,0:T(8,128)(2,1)S(1)} %fusion.11, bf16[1,2048,2048]{2,1,0:T(8,128)(2,1)} %param.23), kind=kOutput, calls=%fused_computation.9 | convolution fusion | flops 134250496 | bytes 8585216 | tf_op jit(solution)/shard_map/dot_general | solution.py:186
  51.4 3.6 %convolution_multiply_fusion.5 = f32[3,3,3,64,64]{4,3,2,1,0:T(8,128)} fusion(bf16[16,4,4,8,64]{4,0,3,2,1:T(8,128)(2,1)S(1)} %multiply_convert_fusion, f32[16,4,4,8,64]{4,0,3,2,1:T(8,128)S(1)} %convolution_multiply_fusion.4), kind=kOutput, calls=%fused_computation.16 | convolution fusion | flops 289124352 | bytes 1228800 | tf_op jit(solution)/shard_map/transpose | solution.py:156
  55.1 5.4 %all-gather = bf16[32,2048]{1,0:T(8,128)(2,1)} all-gather(bf16[16,2048]{1,0:T(8,128)(2,1)S(1)} %copy-done.5), channel_id=2, replica_groups=mesh['wall'=8,'stream_0'=8,'stream_1'=2,'stream_2'=2] {'stream_1'}, dimensions={0}, use_global_device_ids=true | all-gather | bytes 196608 | tf_op jit(solution)/shard_map/all_gather | solution.py:76
  61.2 6.4 %collective-permute-start = (f32[3,8,1,128]{3,2,1,0:T(1,128)}, f32[3,8,1,128]{3,2,1,0:T(1,128)}, u32[]{:S(2)}, u32[]{:S(2)}) collective-permute-start(f32[3,8,1,128]{3,2,1,0:T(1,128)} %get-tuple-element.96), channel_id=1, source_target_pairs={{0,1},{1,2},{2,3},{3,4},{4,5},{5,6},{6,7},{7,8},{8,9},{9,10},{10,1... | collective-permute-start | bytes 36872 | tf_op jit(solution)/shard_map/ppermute | solution.py:45
  69.2 1.3 slice_add_fusion.5
  71.3 1.4 collective-permute-done.1
  72.8 1.3 slice_add_fusion.4
  74.8 1.7 fusion.20
  76.5 52.2 %all-reduce.5.cloned.1.call-done = f32[27,64,64]{2,1,0:T(8,128)} async-done(((f32[27,64,64]{2,1,0:T(8,128)}), f32[27,64,64]{2,1,0:T(8,128)}) %all-reduce.5.cloned.1.call-update) | async-done | bytes 442384 | tf_op jit(solution)/shard_map/psum | solution.py:28
  128.9 5.3 %convolution_multiply_fusion.6 = f32[3,3,3,2,64]{4,3,2,1,0:T(2,128)S(1)} fusion(bf16[16,2,4,4,8]{0,4,3,2,1:T(8,128)(2,1)} %bitcast.141, bf16[16,4,4,8,64]{4,0,3,2,1:T(8,128)(2,1)S(1)} %multiply_convert_fusion, bf16[3,3,3,64,64]{4,3,2,1,0:T(8,128)(2,1)} %bitcast.138, f32[16,4,4,8,64]{4,0,3,2,1:T(8,128)S(1)} %convolution_multiply_fusion.4), kind=kOutput, calls=%fused_computation.20 | convolution fusion | flops 298683776 | bytes 1029632 | tf_op jit(solution)/shard_map/transpose | solution.py:156
  134.2 32.9 %all-gather.6.cloned.1.call-done = bf16[16,16,2048]{2,1,0:T(8,128)(2,1)} async-done(((bf16[2,16,2048]{2,1,0:T(8,128)(2,1)}), bf16[16,16,2048]{2,1,0:T(8,128)(2,1)}) %all-gather.6.cloned.1.call-update) | async-done | bytes 1048592 | tf_op jit(solution)/shard_map/all_gather | solution.py:76
  168.0 4.9 %all-to-all-start.1 = ((f32[8,2,2]{1,2,0:T(2,128)}), f32[8,2,2]{1,2,0:T(2,128)S(1)}, u32[]{:S(2)}, u32[]{:S(2)}) async-start(f32[8,2,2]{1,2,0:T(2,128)} %copy.77), calls=%async_computation.1 | async-start | bytes 16384 | tf_op jit(solution)/shard_map/all_to_all | solution.py:278
  172.9 23.0 %all-reduce = (f32[54,64]{1,0:T(8,128)S(1)}, f32[2048,2]{0,1:T(2,128)S(1)}) all-reduce(f32[54,64]{1,0:T(8,128)S(1)} %reshape.304, f32[2048,2]{0,1:T(2,128)S(1)} %convolution_multiply_fusion.1), channel_id=1, replica_groups=mesh['wall'=8,'stream_0'=8,'stream_1'=2,'stream_2'=2] {'stream_0'}, use_global_device_ids=true, to_apply=%region_5.6 | all-reduce | flops 7552 | bytes 60416 | tf_op jit(solution)/shard_map/psum | solution.py:28
  195.9 24.9 %all-reduce.1 = (f32[54,64]{1,0:T(8,128)S(1)}, f32[2048,2]{0,1:T(2,128)S(1)}) all-reduce(f32[54,64]{1,0:T(8,128)S(1)} %get-tuple-element.84, f32[2048,2]{0,1:T(2,128)S(1)} %get-tuple-element.85), channel_id=1, replica_groups=mesh['wall'=8,'stream_0'=8,'stream_1'=2,'stream_2'=2] {'stream_1','strea..., use_global_device_ids=true, to_apply=%region_6.7 | all-reduce | flops 7552 | bytes 60416 | tf_op jit(solution)/shard_map/psum | solution.py:28
  224.3 8.5 %all-to-all-start.2 = ((bf16[32,2,512]{2,1,0:T(2,128)(2,1)}), bf16[32,2,512]{2,1,0:T(2,128)(2,1)S(1)}, u32[]{:S(2)}, u32[]{:S(2)}) async-start(bf16[32,2,512]{2,1,0:T(2,128)(2,1)} %reshape.333), calls=%async_computation.2 | async-start | bytes 131072 | tf_op jit(solution)/shard_map/all_to_all | solution.py:283
  233.7 9.0 %all-to-all-done.2 = bf16[32,2,512]{2,1,0:T(2,128)(2,1)S(1)} async-done(((bf16[32,2,512]{2,1,0:T(2,128)(2,1)}), bf16[32,2,512]{2,1,0:T(2,128)(2,1)S(1)}, u32[]{:S(2)}, u32[]{:S(2)}) %all-to-all-start.2) | async-done | bytes 65568 | tf_op jit(solution)/shard_map/all_to_all | solution.py:283
  242.8 1.5 multiply_reduce_fusion
  244.3 2.4 fusion.15
  246.7 1.7 copy.82
  249.1 1.9 fusion.16
  (132 shorter events, 21.0 us)
Async XLA Ops:
  7.2 21.4 %copy-start.10 = (bf16[1,54,64]{2,1,0:T(8,128)(2,1)S(1)}, bf16[1,54,64]{2,1,0:T(8,128)(2,1)}, u32[]{:S(2)}) copy-start(bf16[1,54,64]{2,1,0:T(8,128)(2,1)} %param.21) | copy-start | bytes 20740
  7.2 28.5 %copy-start.2 = (bf16[1,27,64,64]{3,2,1,0:T(8,128)(2,1)S(1)}, bf16[1,27,64,64]{3,2,1,0:T(8,128)(2,1)}, u32[]{:S(2)}) copy-start(bf16[1,27,64,64]{3,2,1,0:T(8,128)(2,1)} %param.22) | copy-start | bytes 663556
  8.0 13.8 %collective-permute-start.2 = (f32[3,1,16,128]{3,2,1,0:T(8,128)S(1)}, f32[3,1,16,128]{3,2,1,0:T(8,128)S(1)}, u32[]{:S(2)}, u32[]{:S(2)}) collective-permute-start(f32[3,1,16,128]{3,2,1,0:T(8,128)S(1)} %get-tuple-element.98), channel_id=1, source_target_pairs={{0,32},{32,64},{64,96},{96,128},{128,160},{160,192},{192,224},{224... | collective-permute-start | bytes 73736 | tf_op jit(solution)/shard_map/ppermute | solution.py:45
  10.0 11.8 %collective-permute-start.3 = (f32[3,1,16,128]{3,2,1,0:T(8,128)S(1)}, f32[3,1,16,128]{3,2,1,0:T(8,128)S(1)}, u32[]{:S(2)}, u32[]{:S(2)}) collective-permute-start(f32[3,1,16,128]{3,2,1,0:T(8,128)S(1)} %get-tuple-element.97), channel_id=1, source_target_pairs={{32,0},{64,32},{96,64},{128,96},{160,128},{192,160},{224,192},{0,2... | collective-permute-start | bytes 73736 | tf_op jit(solution)/shard_map/ppermute | solution.py:46
  18.3 17.4 %copy-start.21 = (s32[8]{0:T(128)}, s32[8]{0:T(128)S(1)}, u32[]{:S(2)}) copy-start(s32[8]{0:T(128)S(1)} %multiply_add_fusion) | copy-start | bytes 100
  25.0 8.3 %all-to-all-start = ((bf16[8,2,259]{2,1,0:T(2,128)(2,1)}), bf16[8,2,259]{2,1,0:T(2,128)(2,1)S(1)}, u32[]{:S(2)}, u32[]{:S(2)}) async-start(bf16[8,2,259]{2,1,0:T(2,128)(2,1)} %pad_maximum_fusion.2), calls=%async_computation | async-start | bytes 24576 | tf_op jit(solution)/shard_map/all_to_all | solution.py:62
  28.3 100.4 %all-reduce.5.cloned.1.call-start = ((), (), s32[]{:S(2)}) async-start(), calls=%async_computation.3 | async-start | bytes 1769472 | tf_op jit(solution)/shard_map/psum | solution.py:28
  34.8 4.0 %copy-start.8 = (bf16[16,256]{0,1:T(8,128)(2,1)}, bf16[16,256]{0,1:T(8,128)(2,1)S(1)}, u32[]{:S(2)}) copy-start(bf16[16,256]{0,1:T(8,128)(2,1)S(1)} %copy.74) | copy-start | bytes 24580
  38.9 5.0 %copy-start.13 = (bf16[1,2048,2]{1,2,0:T(2,128)(2,1)S(1)}, bf16[1,2048,2]{1,2,0:T(2,128)(2,1)}, u32[]{:S(2)}) copy-start(bf16[1,2048,2]{1,2,0:T(2,128)(2,1)} %param.24) | copy-start | bytes 24580
  39.0 5.6 %copy-start.17 = (f32[16]{0:T(128)S(1)}, f32[16]{0:T(128)}, u32[]{:S(2)}) copy-start(f32[16]{0:T(128)} %convert_reduce_fusion) | copy-start | bytes 196
  39.3 5.5 %copy-start.19 = (bf16[16,2]{0,1:T(2,128)(2,1)}, bf16[16,2]{0,1:T(2,128)(2,1)S(1)}, u32[]{:S(2)}) copy-start(bf16[16,2]{0,1:T(2,128)(2,1)S(1)} %copy.88) | copy-start | bytes 196
  43.9 7.0 %copy-start.1 = (f32[16,4,4,8,64]{4,0,3,2,1:T(8,128)S(1)}, f32[16,4,4,8,64]{4,0,3,2,1:T(8,128)}, u32[]{:S(2)}) copy-start(f32[16,4,4,8,64]{4,0,3,2,1:T(8,128)} %get-tuple-element.100) | copy-start | bytes 1572868
  44.1 6.8 %copy-start.15 = (f32[16,2]{0,1:T(2,128)}, f32[16,2]{0,1:T(2,128)S(1)}, u32[]{:S(2)}) copy-start(f32[16,2]{0,1:T(2,128)S(1)} %convolution_multiply_fusion.7) | copy-start | bytes 388
  44.8 6.1 %copy-start.4 = (bf16[16,2048]{1,0:T(8,128)(2,1)}, bf16[16,2048]{1,0:T(8,128)(2,1)S(1)}, u32[]{:S(2)}) copy-start(bf16[16,2048]{1,0:T(8,128)(2,1)S(1)} %fusion.11) | copy-start | bytes 196612
  50.9 9.6 %copy-start = (f32[3,8,16,128]{3,2,1,0:T(8,128)S(1)}, f32[3,8,16,128]{3,2,1,0:T(8,128)}, u32[]{:S(2)}) copy-start(f32[3,8,16,128]{3,2,1,0:T(8,128)} %param.18) | copy-start | bytes 589828
  51.3 3.7 %copy-start.5 = (bf16[16,2048]{1,0:T(8,128)(2,1)S(1)}, bf16[16,2048]{1,0:T(8,128)(2,1)}, u32[]{:S(2)}) copy-start(bf16[16,2048]{1,0:T(8,128)(2,1)} %copy-done.4) | copy-start | bytes 196612
  51.3 16.2 %copy-start.12 = (f32[32,16,1,1]{0,1,3,2:T(8,128)S(1)}, f32[32,16,1,1]{0,1,3,2:T(8,128)}, u32[]{:S(2)}) copy-start(f32[32,16,1,1]{0,1,3,2:T(8,128)} %constant.248) | copy-start | bytes 6148
  51.4 16.7 %copy-start.9 = (f32[256,128,1,1]{1,0,3,2:T(8,128)S(1)}, f32[256,128,1,1]{1,0,3,2:T(8,128)}, u32[]{:S(2)}) copy-start(f32[256,128,1,1]{1,0,3,2:T(8,128)} %constant.250) | copy-start | bytes 393220
  55.0 112.1 %all-gather.6.cloned.1.call-start = ((), (), s32[]{:S(2)}) async-start(), calls=%async_computation.5 | async-start | bytes 1179648 | tf_op jit(solution)/shard_map/all_gather | solution.py:76
  60.5 182.3 %all-reduce.7.cloned.1.call-start = ((), (), s32[]{:S(2)}) async-start(), calls=%async_computation.4 | async-start | bytes 1769472 | tf_op jit(solution)/shard_map/psum | solution.py:28
  61.2 8.0 %collective-permute-start = (f32[3,8,1,128]{3,2,1,0:T(1,128)}, f32[3,8,1,128]{3,2,1,0:T(1,128)}, u32[]{:S(2)}, u32[]{:S(2)}) collective-permute-start(f32[3,8,1,128]{3,2,1,0:T(1,128)} %get-tuple-element.96), channel_id=1, source_target_pairs={{0,1},{1,2},{2,3},{3,4},{4,5},{5,6},{6,7},{7,8},{8,9},{9,10},{10,1... | collective-permute-start | bytes 36872 | tf_op jit(solution)/shard_map/ppermute | solution.py:45
  67.5 5.2 %collective-permute-start.1 = (f32[3,8,1,128]{3,2,1,0:T(1,128)}, f32[3,8,1,128]{3,2,1,0:T(1,128)}, u32[]{:S(2)}, u32[]{:S(2)}) collective-permute-start(f32[3,8,1,128]{3,2,1,0:T(1,128)} %get-tuple-element.95), channel_id=1, source_target_pairs={{1,0},{2,1},{3,2},{4,3},{5,4},{6,5},{7,6},{8,7},{9,8},{10,9},{11,1... | collective-permute-start | bytes 36872 | tf_op jit(solution)/shard_map/ppermute | solution.py:46
  128.7 38.4 %copy-start.7 = (bf16[16,2048]{1,0:T(8,128)(2,1)S(1)}, bf16[16,2048]{1,0:T(8,128)(2,1)}, u32[]{:S(2)}) copy-start(bf16[16,2048]{1,0:T(8,128)(2,1)} %copy-done.6) | copy-start | bytes 196612
  128.7 38.4 %copy-start.16 = (f32[16,2]{0,1:T(2,128)S(1)}, f32[16,2]{0,1:T(2,128)}, u32[]{:S(2)}) copy-start(f32[16,2]{0,1:T(2,128)} %copy-done.15) | copy-start | bytes 388
  128.8 38.4 %copy-start.18 = (f32[16]{0:T(128)S(1)}, f32[16]{0:T(128)}, u32[]{:S(2)}) copy-start(f32[16]{0:T(128)} %convert_reduce_fusion) | copy-start | bytes 196
  128.8 38.4 %copy-start.20 = (bf16[16,2]{0,1:T(2,128)(2,1)S(1)}, bf16[16,2]{0,1:T(2,128)(2,1)}, u32[]{:S(2)}) copy-start(bf16[16,2]{0,1:T(2,128)(2,1)} %copy-done.19) | copy-start | bytes 196
  128.8 94.2 %copy-start.14 = (bf16[1,2048,2]{1,2,0:T(2,128)(2,1)S(1)}, bf16[1,2048,2]{1,2,0:T(2,128)(2,1)}, u32[]{:S(2)}) copy-start(bf16[1,2048,2]{1,2,0:T(2,128)(2,1)} %param.24) | copy-start | bytes 24580
  128.8 104.1 %copy-start.22 = (s32[8]{0:T(128)S(1)}, s32[8]{0:T(128)}, u32[]{:S(2)}) copy-start(s32[8]{0:T(128)} %copy-done.21) | copy-start | bytes 100
  128.8 115.5 %copy-start.3 = (bf16[1,27,64,64]{3,2,1,0:T(8,128)(2,1)S(1)}, bf16[1,27,64,64]{3,2,1,0:T(8,128)(2,1)}, u32[]{:S(2)}) copy-start(bf16[1,27,64,64]{3,2,1,0:T(8,128)(2,1)} %param.22) | copy-start | bytes 663556
  128.8 117.9 %all-gather.8.cloned.1.call-start = ((), (), s32[]{:S(2)}) async-start(), calls=%async_computation.6 | async-start | bytes 3145728 | tf_op jit(solution)/shard_map/all_gather | solution.py:76
  168.0 56.4 %all-to-all-start.1 = ((f32[8,2,2]{1,2,0:T(2,128)}), f32[8,2,2]{1,2,0:T(2,128)S(1)}, u32[]{:S(2)}, u32[]{:S(2)}) async-start(f32[8,2,2]{1,2,0:T(2,128)} %copy.77), calls=%async_computation.1 | async-start | bytes 16384 | tf_op jit(solution)/shard_map/all_to_all | solution.py:278
  224.3 18.3 %all-to-all-start.2 = ((bf16[32,2,512]{2,1,0:T(2,128)(2,1)}), bf16[32,2,512]{2,1,0:T(2,128)(2,1)S(1)}, u32[]{:S(2)}, u32[]{:S(2)}) async-start(bf16[32,2,512]{2,1,0:T(2,128)(2,1)} %reshape.333), calls=%async_computation.2 | async-start | bytes 131072 | tf_op jit(solution)/shard_map/all_to_all | solution.py:283
  (2 other events, 4.1 us)
Sparse Core Ops, SparseCore 0:
  55.1 73.5 all-reduce.4
  130.6 36.3 all-gather.5
  169.9 53.2 all-reduce.6
  225.1 16.0 all-gather.7
